TPU v7x, 256 devices: a whole 4x4x8 slice. The times are simulated.
256 devices in a mesh: curve: 16 (over y, x), line: 16 (over z, core).
Axes of the slice: x: 4, y: 4, z: 8, core: 2. Of those that a mesh axis runs over, the one named last changes fastest.
Arguments:
- scaled_distributions: float32 [16, 16, 6, 27, 512], P('curve', 'line'), may hold values from 0.1 to 2.5, as said below
- remaining_brick_places: int32 [16, 16, 6], P('curve', 'line'), may hold values from -1 to 7, as said below
- retained_wavenumbers: int32 [8], replicated, may hold values from 1 to 16, as said below
- regional_amplitudes: float32 [3, 2, 512, 16], P(None, None, 'curve'), may hold values from -0.12 to 0.12
- relaxation_frequencies: float32 [27], replicated, may hold values from 0.6 to 1.8
Outputs:
- new_populations: float32 [16, 16, 6, 27, 512], P('curve', 'line')
Inputs may be any that keep to these rules, and one draw needn't show every extreme that they name: `scaled_distributions`: positive values. `remaining_brick_places`: distinct tile positions (row of the block times 4 plus its column) of one device's surviving blocks, -1 in empty slots, which may stand anywhere; at least half of each device's slots are used, and on some device all 6 are. `retained_wavenumbers`: distinct mode numbers; 16 is always among them.
All inputs are finite; a program needn't handle non-finite values.
Results may differ from a plain program's by a relative error of at most 0.0003.
Values sent between devices are 32-bit elements; how exact they have to be, the bound alone decides.
No kernel may reach another device: no remote copies, remote signals or barrier semaphores. Data moves between devices by JAX's collectives and lax.ppermute only.
A program may use at most 64 MiB of HBM per device.

v0:
```python
import jax
import jax.numpy as jnp
import numpy as np
from jax import lax
from jax.sharding import PartitionSpec as P

BE = 16
TX = 4
TY = 2
NUDGE_GAIN = 0.5
TWO_PI = 6.283185307179586
HIGHEST = lax.Precision.HIGHEST


def with_halo(block, sides, width):
    for axis, dim in sides:
        count = lax.axis_size(axis)
        forward = [(i, i + 1) for i in range(count - 1)]
        forward.append((count - 1, 0))
        backward = [(target, source) for source, target in forward]
        low = lax.ppermute(
            lax.slice_in_dim(block, block.shape[dim] - width, None, axis=dim), axis, forward
        )
        high = lax.ppermute(lax.slice_in_dim(block, 0, width, axis=dim), axis, backward)
        block = jnp.concatenate([low, block, high], axis=dim)
    return block


def lattice_tables():
    one_weights = np.array([1.0 / 6.0, 2.0 / 3.0, 1.0 / 6.0])
    speeds = np.array(
        [
            [along_x - 1, along_y - 1, along_z - 1]
            for along_x in range(3)
            for along_y in range(3)
            for along_z in range(3)
        ]
    )
    weights = np.array(
        [
            one_weights[along_x] * one_weights[along_y] * one_weights[along_z]
            for along_x in range(3)
            for along_y in range(3)
            for along_z in range(3)
        ]
    )
    vander = np.array([[1.0, 1.0, 1.0], [-1.0, 0.0, 1.0], [1.0, 0.0, 1.0]])
    undo_vander = np.array([[0.0, -0.5, 0.5], [1.0, 0.0, -1.0], [0.0, 0.5, 0.5]])
    moment_matrix = np.kron(vander, np.kron(vander, vander))
    inverse = np.kron(undo_vander, np.kron(undo_vander, undo_vander))
    forward = jnp.asarray(moment_matrix * weights[None, :], dtype=jnp.float32)
    backward = jnp.asarray(inverse / weights[:, None], dtype=jnp.float32)
    return (forward, backward, speeds)


def mode_basis_at(mode_ids, positions, length):
    phase_ids = positions[:, None] * mode_ids[None, :] % length
    angles = phase_ids.astype(jnp.float32) * (TWO_PI / length)
    return jnp.concatenate([jnp.cos(angles), jnp.sin(angles)], axis=1)


def tile_velocity(moments, safe_density):
    return jnp.stack([moments[9], moments[3], moments[1]], axis=0) / safe_density[None]


def collide_tile(moments, velocity, nudge_tile, backward, relaxation_frequencies):
    density = moments[0]
    shifted = velocity + nudge_tile
    powers = jnp.stack([jnp.ones_like(shifted), shifted, shifted * shifted + 1.0 / 3.0], axis=0)
    equilibrium = (
        density[None, None, None]
        * powers[:, None, None, 0]
        * powers[None, :, None, 1]
        * powers[None, None, :, 2]
    )
    equilibrium = equilibrium.reshape(moments.shape)
    relaxed = moments - relaxation_frequencies[:, None, None, None] * (moments - equilibrium)
    return jnp.einsum("ij,jlrc->ilrc", backward, relaxed, precision=HIGHEST)


def slot_lookup(living_brick_keys, tile_blocks):
    positions = jnp.arange(tile_blocks, dtype=jnp.int32)
    matches = living_brick_keys[None, :] == positions[:, None]
    slot_numbers = jnp.arange(living_brick_keys.shape[0], dtype=jnp.int32)
    slot_of = jnp.sum(jnp.where(matches, slot_numbers[None, :], 0), axis=1)
    present = jnp.any(matches, axis=1)
    return (slot_of, present)


def compact_to_tile(packed_arrangement, slot_of, present, rows_blocks, cols_blocks, block_edge):
    channels = packed_arrangement.shape[1]
    levels = packed_arrangement.shape[2] // (block_edge * block_edge)
    picked = jnp.take(packed_arrangement, slot_of, axis=0) * present[:, None, None].astype(
        packed_arrangement.dtype
    )
    shaped = picked.reshape(rows_blocks, cols_blocks, channels, levels, block_edge, block_edge)
    return shaped.transpose(2, 3, 0, 4, 1, 5).reshape(
        channels, levels, rows_blocks * block_edge, cols_blocks * block_edge
    )


def tile_to_compact(tile_data, living_brick_keys, rows_blocks, cols_blocks, block_edge):
    channels = tile_data.shape[0]
    levels = tile_data.shape[1]
    shaped = tile_data.reshape(
        channels, levels, rows_blocks, block_edge, cols_blocks, block_edge
    ).transpose(2, 4, 0, 1, 3, 5)
    blocks = shaped.reshape(rows_blocks * cols_blocks, channels, levels * block_edge * block_edge)
    occupied_seats = living_brick_keys >= 0
    picked = jnp.take(blocks, jnp.maximum(living_brick_keys, 0), axis=0)
    return picked * occupied_seats[:, None, None].astype(tile_data.dtype)


def on_device(
    scaled_distributions,
    remaining_brick_places,
    retained_wavenumbers,
    regional_amplitudes,
    relaxation_frequencies,
):
    forward, backward, speeds = lattice_tables()
    slot_state = scaled_distributions[0, 0]
    living_brick_keys = remaining_brick_places[0, 0]
    rows_tile = TY * BE
    cols_tile = TX * BE
    slot_of, present = slot_lookup(living_brick_keys, TX * TY)
    fluid_map = present.reshape(TY, TX).astype(jnp.float32)
    fluid_map = jnp.repeat(jnp.repeat(fluid_map, BE, axis=0), BE, axis=1)
    solid_tile = 1.0 - fluid_map
    pops_tile = compact_to_tile(slot_state, slot_of, present, TY, TX, BE)
    moments = jnp.einsum("ij,jlrc->ilrc", forward, pops_tile, precision=HIGHEST)
    safe_density = jnp.where(fluid_map[None] > 0.5, moments[0], 1.0)
    wind_tile = tile_velocity(moments, safe_density)
    line_length = lax.axis_size("line") * cols_tile
    own_columns = lax.axis_index("line") * cols_tile + jnp.arange(cols_tile, dtype=jnp.int32)
    mode_basis = mode_basis_at(retained_wavenumbers, own_columns, line_length)
    partial = jnp.einsum("klrx,xm->klrm", wind_tile, mode_basis, precision=HIGHEST)
    coefficients = lax.psum(partial, "line")
    misfit = regional_amplitudes - 2.0 / line_length * coefficients
    nudge_tile = NUDGE_GAIN * jnp.einsum("klrm,xm->klrx", misfit, mode_basis, precision=HIGHEST)
    post_tile = collide_tile(moments, wind_tile, nudge_tile, backward, relaxation_frequencies)
    levels = post_tile.shape[1]
    solid_plane = jnp.broadcast_to(solid_tile[None, None], (1, levels, rows_tile, cols_tile))
    extended = jnp.concatenate([post_tile, solid_plane], axis=0)
    padded = with_halo(extended, (("curve", 2), ("line", 3)), 1)
    pops_pad = padded[:27]
    solid_pad = padded[27, 0]
    read = []
    for discrete_heading in range(27):
        carry_eastward = int(speeds[discrete_heading, 0])
        carry_northward = int(speeds[discrete_heading, 1])
        step_z = int(speeds[discrete_heading, 2])
        rows_slice = slice(1 - carry_northward, 1 - carry_northward + rows_tile)
        cols_slice = slice(1 - carry_eastward, 1 - carry_eastward + cols_tile)
        carried_sheet = pops_pad[discrete_heading, :, rows_slice, cols_slice]
        blocked = solid_pad[rows_slice, cols_slice] > 0.5
        bounced_distributions = post_tile[26 - discrete_heading]
        if step_z == 0:
            source = carried_sheet
            block_both = jnp.stack([blocked, blocked])
        elif step_z == 1:
            source = jnp.stack([carried_sheet[0], carried_sheet[0]])
            block_both = jnp.stack([jnp.ones_like(blocked), blocked])
        else:
            mirror_sheet = pops_pad[discrete_heading + 2, 1, rows_slice, cols_slice]
            source = jnp.stack([carried_sheet[1], mirror_sheet])
            block_both = jnp.stack([blocked, blocked])
        read.append(jnp.where(block_both, bounced_distributions, source))
    read_tile = jnp.stack(read, axis=0)
    new_state = tile_to_compact(read_tile, living_brick_keys, TY, TX, BE)
    return new_state[None, None]


def solution(mesh):
    return jax.shard_map(
        on_device,
        mesh=mesh,
        in_specs=(
            P("curve", "line", None, None, None),
            P("curve", "line", None),
            P(),
            P(None, None, "curve", None),
            P(),
        ),
        out_specs=P("curve", "line", None, None, None),
        check_vma=False,
    )
```

profile of v0, /device:TPU:14, one launch (start us, length us, event | category | flops | bytes accessed | tf_op | source)
XLA Modules:
  0.0 145.7 jit_solution(17351706727084608125)
XLA Ops:
  4.7 1.0 copy.376
  6.9 1.0 copy.254
  8.0 2.2 %gather.13 = f32[2,4,27,2,16,16]{5,4,3,1,0,2:T(8,128)S(1)} reshape(f32[8,27,512]{2,0,1:T(8,128)} %copy.254) | data formatting | bytes 884736 | tf_op jit(solution)/shard_map/jit(_take)/gather | solution.py:93
  10.2 3.0 %multiply_bitcast_fusion = f32[27,2,2,16,4,16]{5,3,1,4,2,0:T(8,128)} fusion(f32[2,4,27,2,16,16]{5,4,3,1,0,2:T(8,128)S(1)} %gather.13, f32[2,4]{1,0:T(2,128)} %copy-done.17, pred[2,4]{1,0:T(4,128)(4,1)} %compare_and_fusion), kind=kLoop, calls=%fused_computation.2 | loop fusion | flops 221184 | bytes 884776 | tf_op jit(solution)/shard_map/transpose | solution.py:97
  13.1 3.6 %copy.255 = f32[27,2,2,16,4,16]{0,5,4,3,2,1:T(8,128)S(1)} copy(f32[27,2,2,16,4,16]{5,3,1,4,2,0:T(8,128)} %multiply_bitcast_fusion) | data formatting | bytes 884736 | tf_op jit(solution)/shard_map/transpose | solution.py:97
  17.0 5.8 %fusion.60 = f32[27,2,32,64]{3,0,2,1:T(8,128)S(1)} fusion(f32[27,27,1,1]{1,0,3,2:T(8,128)S(1)} %copy-done.15, f32[27,2,32,64]{0,3,2,1:T(8,128)S(1)} %bitcast.163), kind=kOutput, calls=%fused_computation.236 | convolution fusion | flops 35831808 | bytes 887652 | tf_op jit(solution)/shard_map/ij,jlrc->ilrc/dot_general | solution.py:131
  23.5 51.0 %psum.7 = f32[3,2,32,16]{2,3,1,0:T(8,128)S(1)} all-reduce(f32[3,2,32,16]{2,3,1,0:T(8,128)S(1)} %fusion.7), channel_id=1, replica_groups=mesh['curve'=16,'line'=16] {'line'}, use_global_device_ids=true, to_apply=%region_2.3 | all-reduce | flops 3072 | bytes 24576 | tf_op jit(solution)/shard_map/psum | solution.py:138
  75.6 1.5 %fusion.2 = f32[27,2,32,64]{3,0,2,1:T(8,128)S(1)} fusion(f32[27,27,1,1]{1,0,3,2:T(8,128)S(1)} %copy-done.14, f32[27,2,32,64]{3,0,2,1:T(8,128)S(1)} %fusion.60, f32[27,2,32,64]{3,2,1,0:T(8,128)S(1)} %bitcast.164, f32[27]{0:T(128)S(1)} %copy-done.22), kind=kOutput, calls=%fused_computation.7 | convolution fusion | flops 36163584 | bytes 1330128 | tf_op jit(solution)/shard_map/ij,jlrc->ilrc/dot_general | solution.py:78
  77.8 1.6 %collective-permute-start = (f32[28,2,1,64]{3,2,1,0:T(1,128)S(1)}, f32[28,2,1,64]{3,2,1,0:T(1,128)S(1)}, u32[]{:S(2)}, u32[]{:S(2)}) collective-permute-start(f32[28,2,1,64]{3,2,1,0:T(1,128)S(1)} %get-tuple-element.32), channel_id=1, source_target_pairs={{0,16},{16,32},{32,48},{48,64},{64,80},{80,96},{96,112},{112,128},... | collective-permute-start | bytes 43016 | tf_op jit(solution)/shard_map/ppermute | solution.py:21
  80.0 1.7 %collective-permute-done = f32[28,2,1,64]{3,2,1,0:T(1,128)S(1)} collective-permute-done((f32[28,2,1,64]{3,2,1,0:T(1,128)S(1)}, f32[28,2,1,64]{3,2,1,0:T(1,128)S(1)}, u32[]{:S(2)}, u32[]{:S(2)}) %collective-permute-start) | collective-permute-done | bytes 14368 | tf_op jit(solution)/shard_map/ppermute | solution.py:21
  81.7 3.6 %collective-permute-done.1 = f32[28,2,1,64]{3,2,1,0:T(1,128)S(1)} collective-permute-done((f32[28,2,1,64]{3,2,1,0:T(1,128)S(1)}, f32[28,2,1,64]{3,2,1,0:T(1,128)S(1)}, u32[]{:S(2)}, u32[]{:S(2)}) %collective-permute-start.1) | collective-permute-done | bytes 14368 | tf_op jit(solution)/shard_map/ppermute | solution.py:24
  88.7 2.7 %collective-permute-done.2 = f32[28,2,34,1]{2,1,3,0:T(2,128)S(1)} collective-permute-done((f32[28,2,34,1]{2,1,3,0:T(2,128)S(1)}, f32[28,2,34,1]{2,1,3,0:T(2,128)S(1)}, u32[]{:S(2)}, u32[]{:S(2)}) %collective-permute-start.2) | collective-permute-done | bytes 7648 | tf_op jit(solution)/shard_map/ppermute | solution.py:21
  101.9 1.3 fusion.15
  118.5 1.0 copy_dynamic-update-slice_fusion.26
  119.5 0.9 copy_dynamic-update-slice_fusion.25
  120.4 0.9 copy_dynamic-update-slice_fusion.24
  121.3 0.9 copy_dynamic-update-slice_fusion.23
  122.2 0.9 copy_dynamic-update-slice_fusion.22
  123.1 0.9 copy_dynamic-update-slice_fusion.21
  129.6 0.9 copy_dynamic-update-slice_fusion.14
  130.5 0.9 copy_dynamic-update-slice_fusion.13
  138.9 3.6 %reshape.290 = f32[8,27,512]{2,0,1:T(8,128)} reshape(f32[2,4,27,2,16,16]{5,4,3,1,0,2:T(8,128)S(1)} %bitcast.165) | data formatting | bytes 884736 | tf_op jit(solution)/shard_map/reshape | solution.py:108
  142.5 1.3 copy.326
  144.6 1.1 copy.327
  (164 shorter events, 51.7 us)
Async XLA Ops:
  13.1 3.7 %copy-start.20 = (s32[8]{0:T(128)S(1)}, s32[8]{0:T(128)}, u32[]{:S(2)}) copy-start(s32[8]{0:T(128)} %param.9) | copy-start | bytes 100
  13.1 3.7 %copy-start.21 = (s32[64]{0:T(128)S(1)}, s32[64]{0:T(128)}, u32[]{:S(2)}) copy-start(s32[64]{0:T(128)} %iota_add_fusion) | copy-start | bytes 772
  13.1 3.8 %copy-start.15 = (f32[27,27,1,1]{1,0,3,2:T(8,128)S(1)}, f32[27,27,1,1]{1,0,3,2:T(8,128)}, u32[]{:S(2)}) copy-start(f32[27,27,1,1]{1,0,3,2:T(8,128)} %constant.98) | copy-start | bytes 8752
  13.1 9.6 %copy-start.16 = (pred[32,64]{1,0:T(8,128)(4,1)S(1)}, pred[32,64]{1,0:T(8,128)(4,1)}, u32[]{:S(2)}) copy-start(pred[32,64]{1,0:T(8,128)(4,1)} %copy.258) | copy-start | bytes 6148
  13.1 61.4 %copy-start.12 = (f32[3,2,32,16]{2,3,1,0:T(8,128)S(1)}, f32[3,2,32,16]{2,3,1,0:T(8,128)}, u32[]{:S(2)}) copy-start(f32[3,2,32,16]{2,3,1,0:T(8,128)} %param.10) | copy-start | bytes 36868
  16.9 58.7 %copy-start.14 = (f32[27,27,1,1]{1,0,3,2:T(8,128)S(1)}, f32[27,27,1,1]{1,0,3,2:T(8,128)}, u32[]{:S(2)}) copy-start(f32[27,27,1,1]{1,0,3,2:T(8,128)} %constant.97) | copy-start | bytes 8752
  16.9 58.7 %copy-start.22 = (f32[27]{0:T(128)S(1)}, f32[27]{0:T(128)}, u32[]{:S(2)}) copy-start(f32[27]{0:T(128)} %param.11) | copy-start | bytes 328
  77.8 3.9 %collective-permute-start = (f32[28,2,1,64]{3,2,1,0:T(1,128)S(1)}, f32[28,2,1,64]{3,2,1,0:T(1,128)S(1)}, u32[]{:S(2)}, u32[]{:S(2)}) collective-permute-start(f32[28,2,1,64]{3,2,1,0:T(1,128)S(1)} %get-tuple-element.32), channel_id=1, source_target_pairs={{0,16},{16,32},{32,48},{48,64},{64,80},{80,96},{96,112},{112,128},... | collective-permute-start | bytes 43016 | tf_op jit(solution)/shard_map/ppermute | solution.py:21
  79.3 6.0 %collective-permute-start.1 = (f32[28,2,1,64]{3,2,1,0:T(1,128)S(1)}, f32[28,2,1,64]{3,2,1,0:T(1,128)S(1)}, u32[]{:S(2)}, u32[]{:S(2)}) collective-permute-start(f32[28,2,1,64]{3,2,1,0:T(1,128)S(1)} %get-tuple-element.33), channel_id=1, source_target_pairs={{16,0},{32,16},{48,32},{64,48},{80,64},{96,80},{112,96},{128,112},... | collective-permute-start | bytes 43016 | tf_op jit(solution)/shard_map/ppermute | solution.py:24
  86.9 5.1 %collective-permute-start.3 = (f32[28,2,34,1]{2,1,3,0:T(2,128)S(1)}, f32[28,2,34,1]{2,1,3,0:T(2,128)S(1)}, u32[]{:S(2)}, u32[]{:S(2)}) collective-permute-start(f32[28,2,34,1]{2,1,3,0:T(2,128)S(1)} %copy.266), channel_id=1, source_target_pairs={{1,0},{2,1},{3,2},{4,3},{5,4},{6,5},{7,6},{8,7},{9,8},{10,9},{11,1... | collective-permute-start | bytes 22856 | tf_op jit(solution)/shard_map/ppermute | solution.py:24
  86.9 4.5 %collective-permute-start.2 = (f32[28,2,34,1]{2,1,3,0:T(2,128)S(1)}, f32[28,2,34,1]{2,1,3,0:T(2,128)S(1)}, u32[]{:S(2)}, u32[]{:S(2)}) collective-permute-start(f32[28,2,34,1]{2,1,3,0:T(2,128)S(1)} %copy.265), channel_id=1, source_target_pairs={{0,1},{1,2},{2,3},{3,4},{4,5},{5,6},{6,7},{7,8},{8,9},{9,10},{10,1... | collective-permute-start | bytes 22856 | tf_op jit(solution)/shard_map/ppermute | solution.py:21
  105.8 4.1 %copy-start.6 = (f32[2,32,64]{2,1,0:T(8,128)S(1)}, f32[2,32,64]{2,1,0:T(8,128)}, u32[]{:S(2)}) copy-start(f32[2,32,64]{2,1,0:T(8,128)} %get-tuple-element.43) | copy-start | bytes 49156
  105.8 4.9 %copy-start.5 = (f32[2,32,64]{2,1,0:T(8,128)S(1)}, f32[2,32,64]{2,1,0:T(8,128)}, u32[]{:S(2)}) copy-start(f32[2,32,64]{2,1,0:T(8,128)} %get-tuple-element.44) | copy-start | bytes 49156
  105.8 8.7 %copy-start.10 = (f32[1,2,32,64]{3,2,1,0:T(8,128)S(1)}, f32[1,2,32,64]{3,2,1,0:T(8,128)}, u32[]{:S(2)}) copy-start(f32[1,2,32,64]{3,2,1,0:T(8,128)} %get-tuple-element.25) | copy-start | bytes 49156
  105.8 10.3 %copy-start.9 = (f32[2,32,64]{2,1,0:T(8,128)S(1)}, f32[2,32,64]{2,1,0:T(8,128)}, u32[]{:S(2)}) copy-start(f32[2,32,64]{2,1,0:T(8,128)} %get-tuple-element.38) | copy-start | bytes 49156
  105.9 11.0 %copy-start.8 = (f32[2,32,64]{2,1,0:T(8,128)S(1)}, f32[2,32,64]{2,1,0:T(8,128)}, u32[]{:S(2)}) copy-start(f32[2,32,64]{2,1,0:T(8,128)} %get-tuple-element.39) | copy-start | bytes 49156
  105.9 11.8 %copy-start.7 = (f32[2,32,64]{2,1,0:T(8,128)S(1)}, f32[2,32,64]{2,1,0:T(8,128)}, u32[]{:S(2)}) copy-start(f32[2,32,64]{2,1,0:T(8,128)} %get-tuple-element.40) | copy-start | bytes 49156
  118.5 12.9 %copy-start.4 = (f32[1,2,2,16,4,16]{5,4,3,2,1,0:T(4,128)S(1)}, f32[1,2,2,16,4,16]{5,4,3,2,1,0:T(4,128)}, u32[]{:S(2)}) copy-start(f32[1,2,2,16,4,16]{5,4,3,2,1,0:T(4,128)} %stack.342) | copy-start | bytes 49156
  118.5 13.0 %copy-start.3 = (f32[1,2,2,16,4,16]{5,4,3,2,1,0:T(4,128)S(1)}, f32[1,2,2,16,4,16]{5,4,3,2,1,0:T(4,128)}, u32[]{:S(2)}) copy-start(f32[1,2,2,16,4,16]{5,4,3,2,1,0:T(4,128)} %stack.346) | copy-start | bytes 49156
  118.5 13.9 %copy-start.2 = (f32[1,2,2,16,4,16]{5,4,3,2,1,0:T(4,128)S(1)}, f32[1,2,2,16,4,16]{5,4,3,2,1,0:T(4,128)}, u32[]{:S(2)}) copy-start(f32[1,2,2,16,4,16]{5,4,3,2,1,0:T(4,128)} %stack.351) | copy-start | bytes 49156
  118.5 14.9 %copy-start = (f32[1,2,2,16,4,16]{5,4,3,2,1,0:T(4,128)S(1)}, f32[1,2,2,16,4,16]{5,4,3,2,1,0:T(4,128)}, u32[]{:S(2)}) copy-start(f32[1,2,2,16,4,16]{5,4,3,2,1,0:T(4,128)} %stack.356) | copy-start | bytes 49156
  118.5 14.9 %copy-start.1 = (f32[1,2,2,16,4,16]{5,4,3,2,1,0:T(4,128)S(1)}, f32[1,2,2,16,4,16]{5,4,3,2,1,0:T(4,128)}, u32[]{:S(2)}) copy-start(f32[1,2,2,16,4,16]{5,4,3,2,1,0:T(4,128)} %stack.360) | copy-start | bytes 49156
  134.3 10.2 %copy-start.18 = (pred[6]{0:T(512)(128)(4,1)S(1)}, pred[6]{0:T(512)(128)(4,1)}, u32[]{:S(2)}) copy-start(pred[6]{0:T(512)(128)(4,1)} %get-tuple-element.62) | copy-start | bytes 22
  134.3 10.2 %copy-start.19 = (f32[6]{0:T(128)S(1)}, f32[6]{0:T(128)}, u32[]{:S(2)}) copy-start(f32[6]{0:T(128)} %get-tuple-element.63) | copy-start | bytes 76
  (4 other events, 8.0 us)
where the time goes:
time: 146 us
  local copies, waits for them, and re-layouts  61 us (42%)
  blocking collectives  51 us (35%)
  other arithmetic  14.3 us (10%)
  matrix products  8.15 us (6%)
  waiting for transfers between devices  7.99 us (5%)
  starting transfers between devices  2.62 us (2%)
    psum x1, blocking collectives, on_device(): coefficients = lax.psum(partial, 'line')  51 us
    another operation x28, local copies, waits for them, and re-layouts, on_device(): read_tile = jnp.stack(read, axis=0)  21.8 us
    unnamed x75, local copies, waits for them, and re-layouts  20.5 us
    dot_general x1, matrix products, on_device(): moments = jnp.einsum('ij,jlrc->ilrc', forward, pops_tile, precision=HIGHEST)  5.79 us
    reshape x2, local copies, waits for them, and re-layouts, tile_to_compact(): shaped.reshape(rows_blocks * cols_blocks, channels, levels * block_edge *...  4.88 us
    ppermute x2, waiting for transfers between devices, with_halo(): lax.ppermute(lax.slice_in_dim(block, block.shape[dim] - width, None, axis...  4.39 us
    select_n x14, other arithmetic, on_device(): read.append(jnp.where(block_both, bounced_distributions, source))  4.2 us
    gather x3, local copies, waits for them, and re-layouts, compact_to_tile(): jnp.take(packed_arrangement, slot_of, axis=0)  3.8 us
  transfers between devices with their start and end apart: 4, of which 3 were waited for; matrix products, arithmetic and copies ran while one was open for 1% of the time, Pallas kernels for 0%

commit v1 on v0

--- a/solution.py
+++ b/solution.py
@@ -10,6 +10,12 @@
 NUDGE_GAIN = 0.5
 TWO_PI = 6.283185307179586
 HIGHEST = lax.Precision.HIGHEST
+
+
+def add_all(shard, mesh_axis):
+    shards = lax.all_gather(shard, mesh_axis, axis=0, tiled=False)
+    total = shards.sum(axis=0)
+    return total
 
 
 def with_halo(block, sides, width):
@@ -135,7 +141,7 @@
     own_columns = lax.axis_index("line") * cols_tile + jnp.arange(cols_tile, dtype=jnp.int32)
     mode_basis = mode_basis_at(retained_wavenumbers, own_columns, line_length)
     partial = jnp.einsum("klrx,xm->klrm", wind_tile, mode_basis, precision=HIGHEST)
-    coefficients = lax.psum(partial, "line")
+    coefficients = add_all(partial, "line")
     misfit = regional_amplitudes - 2.0 / line_length * coefficients
     nudge_tile = NUDGE_GAIN * jnp.einsum("klrm,xm->klrx", misfit, mode_basis, precision=HIGHEST)
     post_tile = collide_tile(moments, wind_tile, nudge_tile, backward, relaxation_frequencies)

time: 146 us -> 118 us (0.81)
  blocking collectives: 51 us -> 22.1 us
    psum x1 -> x0, blocking collectives: 51 us -> none  [on_device(): coefficients = lax.psum(partial, 'line')]
    all_gather x0 -> x1, blocking collectives: none -> 22.1 us  [add_all(): shards = lax.all_gather(shard, mesh_axis, axis=0, tiled=False)]
  transfers between devices with their start and end apart: 4 -> 4, of which waited for: 3 -> 3; matrix products, arithmetic and copies ran while one was open for 1% -> 2% of each run, Pallas kernels for 0% -> 0%
where the time goes in v1:
time: 118 us; the launch traced here: 117 us
  local copies, waits for them, and re-layouts  61 us (52%)
  blocking collectives  22.1 us (19%)
  other arithmetic  14.4 us (12%)
  matrix products  8.15 us (7%)
  waiting for transfers between devices  7.99 us (7%)
  starting transfers between devices  2.62 us (2%)
    all_gather x1, blocking collectives, add_all(): shards = lax.all_gather(shard, mesh_axis, axis=0, tiled=False)  22.1 us
    another operation x28, local copies, waits for them, and re-layouts, on_device(): read_tile = jnp.stack(read, axis=0)  21.8 us
    unnamed x75, local copies, waits for them, and re-layouts  20.5 us
    dot_general x1, matrix products, on_device(): moments = jnp.einsum('ij,jlrc->ilrc', forward, pops_tile, precision=HIGHEST)  5.79 us
    reshape x2, local copies, waits for them, and re-layouts, tile_to_compact(): shaped.reshape(rows_blocks * cols_blocks, channels, levels * block_edge *...  4.88 us
    ppermute x2, waiting for transfers between devices, with_halo(): lax.ppermute(lax.slice_in_dim(block, block.shape[dim] - width, None, axis...  4.39 us
    select_n x14, other arithmetic, on_device(): read.append(jnp.where(block_both, bounced_distributions, source))  4.2 us
    gather x3, local copies, waits for them, and re-layouts, compact_to_tile(): jnp.take(packed_arrangement, slot_of, axis=0)  3.8 us
  transfers between devices with their start and end apart: 4, of which 3 were waited for; matrix products, arithmetic and copies ran while one was open for 2% of the time, Pallas kernels for 0%

profile of v1, /device:TPU:14, one launch (start us, length us, event | category | flops | bytes accessed | tf_op | source)
XLA Modules:
  0.0 116.9 jit_solution(10544610866199394814)
XLA Ops:
  4.7 1.0 copy.378
  6.9 1.0 copy.256
  8.0 2.2 %gather.13 = f32[2,4,27,2,16,16]{5,4,3,1,0,2:T(8,128)S(1)} reshape(f32[8,27,512]{2,0,1:T(8,128)} %copy.256) | data formatting | bytes 884736 | tf_op jit(solution)/shard_map/jit(_take)/gather | solution.py:99
  10.2 3.0 %multiply_bitcast_fusion = f32[27,2,2,16,4,16]{5,3,1,4,2,0:T(8,128)} fusion(f32[2,4,27,2,16,16]{5,4,3,1,0,2:T(8,128)S(1)} %gather.13, f32[2,4]{1,0:T(2,128)} %copy-done.17, pred[2,4]{1,0:T(4,128)(4,1)} %compare_and_fusion), kind=kLoop, calls=%fused_computation.2 | loop fusion | flops 221184 | bytes 884776 | tf_op jit(solution)/shard_map/transpose | solution.py:103
  13.1 3.6 %copy.257 = f32[27,2,2,16,4,16]{0,5,4,3,2,1:T(8,128)S(1)} copy(f32[27,2,2,16,4,16]{5,3,1,4,2,0:T(8,128)} %multiply_bitcast_fusion) | data formatting | bytes 884736 | tf_op jit(solution)/shard_map/transpose | solution.py:103
  16.9 5.8 %fusion.60 = f32[27,2,32,64]{3,0,2,1:T(8,128)S(1)} fusion(f32[27,27,1,1]{1,0,3,2:T(8,128)S(1)} %copy-done.15, f32[27,2,32,64]{0,3,2,1:T(8,128)S(1)} %bitcast.164), kind=kOutput, calls=%fused_computation.236 | convolution fusion | flops 35831808 | bytes 887652 | tf_op jit(solution)/shard_map/ij,jlrc->ilrc/dot_general | solution.py:137
  23.5 22.1 %all-gather = f32[48,2,32,16]{2,3,1,0:T(8,128)S(1)} all-gather(f32[3,2,32,16]{2,3,1,0:T(8,128)S(1)} %fusion.7), channel_id=2, replica_groups=mesh['curve'=16,'line'=16] {'line'}, dimensions={0}, use_global_device_ids=true | all-gather | bytes 208896 | tf_op jit(solution)/shard_map/all_gather | solution.py:16
  46.9 1.5 %fusion.2 = f32[27,2,32,64]{3,0,2,1:T(8,128)S(1)} fusion(f32[27,27,1,1]{1,0,3,2:T(8,128)S(1)} %copy-done.14, f32[27,2,32,64]{3,0,2,1:T(8,128)S(1)} %fusion.60, f32[27,2,32,64]{3,2,1,0:T(8,128)S(1)} %bitcast.165, f32[27]{0:T(128)S(1)} %copy-done.22), kind=kOutput, calls=%fused_computation.7 | convolution fusion | flops 36163584 | bytes 1330128 | tf_op jit(solution)/shard_map/ij,jlrc->ilrc/dot_general | solution.py:84
  49.0 1.6 %collective-permute-start = (f32[28,2,1,64]{3,2,1,0:T(1,128)S(1)}, f32[28,2,1,64]{3,2,1,0:T(1,128)S(1)}, u32[]{:S(2)}, u32[]{:S(2)}) collective-permute-start(f32[28,2,1,64]{3,2,1,0:T(1,128)S(1)} %get-tuple-element.32), channel_id=1, source_target_pairs={{0,16},{16,32},{32,48},{48,64},{64,80},{80,96},{96,112},{112,128},... | collective-permute-start | bytes 43016 | tf_op jit(solution)/shard_map/ppermute | solution.py:27
  51.2 1.7 %collective-permute-done = f32[28,2,1,64]{3,2,1,0:T(1,128)S(1)} collective-permute-done((f32[28,2,1,64]{3,2,1,0:T(1,128)S(1)}, f32[28,2,1,64]{3,2,1,0:T(1,128)S(1)}, u32[]{:S(2)}, u32[]{:S(2)}) %collective-permute-start) | collective-permute-done | bytes 14368 | tf_op jit(solution)/shard_map/ppermute | solution.py:27
  52.9 3.6 %collective-permute-done.1 = f32[28,2,1,64]{3,2,1,0:T(1,128)S(1)} collective-permute-done((f32[28,2,1,64]{3,2,1,0:T(1,128)S(1)}, f32[28,2,1,64]{3,2,1,0:T(1,128)S(1)}, u32[]{:S(2)}, u32[]{:S(2)}) %collective-permute-start.1) | collective-permute-done | bytes 14368 | tf_op jit(solution)/shard_map/ppermute | solution.py:30
  60.0 2.7 %collective-permute-done.2 = f32[28,2,34,1]{2,1,3,0:T(2,128)S(1)} collective-permute-done((f32[28,2,34,1]{2,1,3,0:T(2,128)S(1)}, f32[28,2,34,1]{2,1,3,0:T(2,128)S(1)}, u32[]{:S(2)}, u32[]{:S(2)}) %collective-permute-start.2) | collective-permute-done | bytes 7648 | tf_op jit(solution)/shard_map/ppermute | solution.py:27
  73.1 1.3 %fusion.15 = (f32[2,32,64]{2,1,0:T(8,128)S(1)}, f32[2,32,64]{2,1,0:T(8,128)}, f32[2,32,64]{2,1,0:T(8,128)}, f32[2,32,64]{2,1,0:T(8,128)}) fusion(f32[27,2,32,64]{3,2,1,0:T(8,128)S(1)} %copy.266, f32[1,32,64]{2,1,0:T(8,128)S(1)} %get-tuple-element.7, pred[1,32,64]{2,1,0:T(8,128)(4,1)S(1)} %bitcast.178, f32[1,32,64]{2,1,0:T(8,128)S(1)} %get-tuple-element.6, ...), kind=kLoop, calls=%fused_computation.66 | loop fusion | flops 32768 | bytes 172032 | tf_op jit(solution)/shard_map/jit(_where)/select_n | solution.py:174
  89.7 1.0 copy_dynamic-update-slice_fusion.26
  90.7 0.9 copy_dynamic-update-slice_fusion.25
  91.6 0.9 copy_dynamic-update-slice_fusion.24
  92.5 0.9 copy_dynamic-update-slice_fusion.23
  93.4 0.9 copy_dynamic-update-slice_fusion.22
  94.4 0.9 copy_dynamic-update-slice_fusion.21
  95.3 0.9 copy_dynamic-update-slice_fusion.20
  102.7 0.9 copy_dynamic-update-slice_fusion.10
  110.1 3.6 %reshape.290 = f32[8,27,512]{2,0,1:T(8,128)} reshape(f32[2,4,27,2,16,16]{5,4,3,1,0,2:T(8,128)S(1)} %bitcast.166) | data formatting | bytes 884736 | tf_op jit(solution)/shard_map/reshape | solution.py:114
  113.8 1.3 %copy.328 = f32[8,27,512]{2,1,0:T(8,128)S(1)} copy(f32[8,27,512]{2,0,1:T(8,128)} %reshape.290) | data formatting | bytes 884736 | tf_op jit(solution)/shard_map/reshape | solution.py:114
  115.9 1.1 copy.329
  (165 shorter events, 51.8 us)
Async XLA Ops:
  13.1 3.6 %copy-start.20 = (s32[8]{0:T(128)S(1)}, s32[8]{0:T(128)}, u32[]{:S(2)}) copy-start(s32[8]{0:T(128)} %param.9) | copy-start | bytes 100
  13.1 3.7 %copy-start.21 = (s32[64]{0:T(128)S(1)}, s32[64]{0:T(128)}, u32[]{:S(2)}) copy-start(s32[64]{0:T(128)} %iota_add_fusion) | copy-start | bytes 772
  13.1 3.8 %copy-start.15 = (f32[27,27,1,1]{1,0,3,2:T(8,128)S(1)}, f32[27,27,1,1]{1,0,3,2:T(8,128)}, u32[]{:S(2)}) copy-start(f32[27,27,1,1]{1,0,3,2:T(8,128)} %constant.100) | copy-start | bytes 8752
  13.1 9.6 %copy-start.16 = (pred[32,64]{1,0:T(8,128)(4,1)S(1)}, pred[32,64]{1,0:T(8,128)(4,1)}, u32[]{:S(2)}) copy-start(pred[32,64]{1,0:T(8,128)(4,1)} %copy.260) | copy-start | bytes 6148
  16.8 28.9 %copy-start.12 = (f32[3,2,32,16]{2,3,1,0:T(8,128)S(1)}, f32[3,2,32,16]{2,3,1,0:T(8,128)}, u32[]{:S(2)}) copy-start(f32[3,2,32,16]{2,3,1,0:T(8,128)} %param.10) | copy-start | bytes 36868
  22.7 24.1 %copy-start.14 = (f32[27,27,1,1]{1,0,3,2:T(8,128)S(1)}, f32[27,27,1,1]{1,0,3,2:T(8,128)}, u32[]{:S(2)}) copy-start(f32[27,27,1,1]{1,0,3,2:T(8,128)} %constant.99) | copy-start | bytes 8752
  22.7 24.1 %copy-start.22 = (f32[27]{0:T(128)S(1)}, f32[27]{0:T(128)}, u32[]{:S(2)}) copy-start(f32[27]{0:T(128)} %param.11) | copy-start | bytes 328
  49.0 3.9 %collective-permute-start = (f32[28,2,1,64]{3,2,1,0:T(1,128)S(1)}, f32[28,2,1,64]{3,2,1,0:T(1,128)S(1)}, u32[]{:S(2)}, u32[]{:S(2)}) collective-permute-start(f32[28,2,1,64]{3,2,1,0:T(1,128)S(1)} %get-tuple-element.32), channel_id=1, source_target_pairs={{0,16},{16,32},{32,48},{48,64},{64,80},{80,96},{96,112},{112,128},... | collective-permute-start | bytes 43016 | tf_op jit(solution)/shard_map/ppermute | solution.py:27
  50.6 6.0 %collective-permute-start.1 = (f32[28,2,1,64]{3,2,1,0:T(1,128)S(1)}, f32[28,2,1,64]{3,2,1,0:T(1,128)S(1)}, u32[]{:S(2)}, u32[]{:S(2)}) collective-permute-start(f32[28,2,1,64]{3,2,1,0:T(1,128)S(1)} %get-tuple-element.33), channel_id=1, source_target_pairs={{16,0},{32,16},{48,32},{64,48},{80,64},{96,80},{112,96},{128,112},... | collective-permute-start | bytes 43016 | tf_op jit(solution)/shard_map/ppermute | solution.py:30
  58.1 5.1 %collective-permute-start.3 = (f32[28,2,34,1]{2,1,3,0:T(2,128)S(1)}, f32[28,2,34,1]{2,1,3,0:T(2,128)S(1)}, u32[]{:S(2)}, u32[]{:S(2)}) collective-permute-start(f32[28,2,34,1]{2,1,3,0:T(2,128)S(1)} %copy.268), channel_id=1, source_target_pairs={{1,0},{2,1},{3,2},{4,3},{5,4},{6,5},{7,6},{8,7},{9,8},{10,9},{11,1... | collective-permute-start | bytes 22856 | tf_op jit(solution)/shard_map/ppermute | solution.py:30
  58.1 4.5 %collective-permute-start.2 = (f32[28,2,34,1]{2,1,3,0:T(2,128)S(1)}, f32[28,2,34,1]{2,1,3,0:T(2,128)S(1)}, u32[]{:S(2)}, u32[]{:S(2)}) collective-permute-start(f32[28,2,34,1]{2,1,3,0:T(2,128)S(1)} %copy.267), channel_id=1, source_target_pairs={{0,1},{1,2},{2,3},{3,4},{4,5},{5,6},{6,7},{7,8},{8,9},{9,10},{10,1... | collective-permute-start | bytes 22856 | tf_op jit(solution)/shard_map/ppermute | solution.py:27
  77.0 4.1 %copy-start.6 = (f32[2,32,64]{2,1,0:T(8,128)S(1)}, f32[2,32,64]{2,1,0:T(8,128)}, u32[]{:S(2)}) copy-start(f32[2,32,64]{2,1,0:T(8,128)} %get-tuple-element.43) | copy-start | bytes 49156
  77.1 4.9 %copy-start.5 = (f32[2,32,64]{2,1,0:T(8,128)S(1)}, f32[2,32,64]{2,1,0:T(8,128)}, u32[]{:S(2)}) copy-start(f32[2,32,64]{2,1,0:T(8,128)} %get-tuple-element.44) | copy-start | bytes 49156
  77.1 8.7 %copy-start.10 = (f32[1,2,32,64]{3,2,1,0:T(8,128)S(1)}, f32[1,2,32,64]{3,2,1,0:T(8,128)}, u32[]{:S(2)}) copy-start(f32[1,2,32,64]{3,2,1,0:T(8,128)} %get-tuple-element.25) | copy-start | bytes 49156
  77.1 10.3 %copy-start.9 = (f32[2,32,64]{2,1,0:T(8,128)S(1)}, f32[2,32,64]{2,1,0:T(8,128)}, u32[]{:S(2)}) copy-start(f32[2,32,64]{2,1,0:T(8,128)} %get-tuple-element.38) | copy-start | bytes 49156
  77.1 11.0 %copy-start.8 = (f32[2,32,64]{2,1,0:T(8,128)S(1)}, f32[2,32,64]{2,1,0:T(8,128)}, u32[]{:S(2)}) copy-start(f32[2,32,64]{2,1,0:T(8,128)} %get-tuple-element.39) | copy-start | bytes 49156
  77.1 11.8 %copy-start.7 = (f32[2,32,64]{2,1,0:T(8,128)S(1)}, f32[2,32,64]{2,1,0:T(8,128)}, u32[]{:S(2)}) copy-start(f32[2,32,64]{2,1,0:T(8,128)} %get-tuple-element.40) | copy-start | bytes 49156
  89.7 12.9 %copy-start.4 = (f32[1,2,2,16,4,16]{5,4,3,2,1,0:T(4,128)S(1)}, f32[1,2,2,16,4,16]{5,4,3,2,1,0:T(4,128)}, u32[]{:S(2)}) copy-start(f32[1,2,2,16,4,16]{5,4,3,2,1,0:T(4,128)} %stack.342) | copy-start | bytes 49156
  89.7 13.0 %copy-start.3 = (f32[1,2,2,16,4,16]{5,4,3,2,1,0:T(4,128)S(1)}, f32[1,2,2,16,4,16]{5,4,3,2,1,0:T(4,128)}, u32[]{:S(2)}) copy-start(f32[1,2,2,16,4,16]{5,4,3,2,1,0:T(4,128)} %stack.346) | copy-start | bytes 49156
  89.7 13.9 %copy-start.2 = (f32[1,2,2,16,4,16]{5,4,3,2,1,0:T(4,128)S(1)}, f32[1,2,2,16,4,16]{5,4,3,2,1,0:T(4,128)}, u32[]{:S(2)}) copy-start(f32[1,2,2,16,4,16]{5,4,3,2,1,0:T(4,128)} %stack.351) | copy-start | bytes 49156
  89.7 14.9 %copy-start = (f32[1,2,2,16,4,16]{5,4,3,2,1,0:T(4,128)S(1)}, f32[1,2,2,16,4,16]{5,4,3,2,1,0:T(4,128)}, u32[]{:S(2)}) copy-start(f32[1,2,2,16,4,16]{5,4,3,2,1,0:T(4,128)} %stack.356) | copy-start | bytes 49156
  89.7 14.9 %copy-start.1 = (f32[1,2,2,16,4,16]{5,4,3,2,1,0:T(4,128)S(1)}, f32[1,2,2,16,4,16]{5,4,3,2,1,0:T(4,128)}, u32[]{:S(2)}) copy-start(f32[1,2,2,16,4,16]{5,4,3,2,1,0:T(4,128)} %stack.360) | copy-start | bytes 49156
  105.5 10.2 %copy-start.18 = (pred[6]{0:T(512)(128)(4,1)S(1)}, pred[6]{0:T(512)(128)(4,1)}, u32[]{:S(2)}) copy-start(pred[6]{0:T(512)(128)(4,1)} %get-tuple-element.62) | copy-start | bytes 22
  105.5 10.2 %copy-start.19 = (f32[6]{0:T(128)S(1)}, f32[6]{0:T(128)}, u32[]{:S(2)}) copy-start(f32[6]{0:T(128)} %get-tuple-element.63) | copy-start | bytes 76
  (4 other events, 8.0 us)
